TPU v7x, 32 devices: a whole 2x2x4 slice. The times are simulated.
32 devices in a mesh: groups: 2 (over y), seq: 4 (over z), tensor: 2 (over x), dp: 2 (over core).
Axes of the slice: x: 2, y: 2, z: 4, core: 2. Of those that a mesh axis runs over, the one named last changes fastest.
Arguments:
- tokens: bfloat16 [4, 1024, 4096], P(('groups', 'dp'), 'seq', 'tensor'), parts along dimension 0, may hold values from -6 to 6
- doc_lengths: int32 [4, 8], P(('groups', 'dp')), parts along dimension 0, may hold values from 1 to 768, 1024 in all within a row
- low_taps: float32 [2, 4096], P(None, 'tensor'), may hold values from 0.66 to 0.75
- high_taps: float32 [2, 4096], P(None, 'tensor'), may hold values from -2.5 to 2.5
- level_weights: float32 [13, 4096], P(None, 'tensor'), may hold values from -2.5 to 2.5
- mix_weight: bfloat16 [4096, 4096], P(None, 'tensor'), may hold values from -0.09375 to 0.09375
- out_grad: bfloat16 [4, 1024, 4096], P(('groups', 'dp'), 'seq', 'tensor'), parts along dimension 0, may hold values from -6 to 6
Outputs:
- result: bfloat16 [4, 1024, 4096], P(('groups', 'dp'), 'seq', 'tensor'), parts along dimension 0
- token_grad: bfloat16 [4, 1024, 4096], P(('groups', 'dp'), 'seq', 'tensor'), parts along dimension 0
- weight_grad: bfloat16 [8192, 4096], P(('groups', 'seq', 'dp'), 'tensor'), parts along dimension 0
- low_grad: float32 [4, 4096], P('groups', 'tensor'), parts along dimension 0
- high_grad: float32 [4, 4096], P('groups', 'tensor'), parts along dimension 0
- level_grad: float32 [26, 4096], P('groups', 'tensor'), parts along dimension 0
There are 2 independent parts, one for each index of `groups`. A program takes and returns all parts, laid end to end along the dimension named above; an argument that names none is the same for every part. Nothing has to cross between parts.
Inputs may be any that keep to these rules, and one draw needn't show every extreme that they name: `doc_lengths`: each row of 8 lengths sums to 1024, and its longest document has exactly 768 positions.
All inputs are finite; a program needn't handle non-finite values.
Results may differ from a plain program's by a relative error of at most 0.015.
Values may be sent and summed in bfloat16 or wider, within the bound.
No kernel may reach another device: no remote copies, remote signals or barrier semaphores. Data moves between devices by JAX's collectives and lax.ppermute only.
A program may use at most 128 MiB of HBM per device.

v0:
```python
import jax
import jax.numpy as jnp
from jax import lax
from jax.sharding import PartitionSpec as P

GELU_SCALE = 0.7978845608028654
GELU_CUBIC = 0.044715


def shifted_2(block, axis, distance):
    devices = range(lax.axis_size(axis))
    route = [(i - distance, i) for i in devices if i - distance in devices]
    return lax.ppermute(block, axis, route)


def gelu_value(values):
    tangent = jnp.tanh(GELU_SCALE * (values + GELU_CUBIC * values * values * values))
    return 0.5 * values * (1.0 + tangent)


def gelu_slope(values):
    tangent = jnp.tanh(GELU_SCALE * (values + GELU_CUBIC * values * values * values))
    return 0.5 * (1.0 + tangent) + 0.5 * values * (1.0 - tangent * tangent) * GELU_SCALE * (
        1.0 + 3.0 * GELU_CUBIC * values * values
    )


def doc_starts(positions, doc_lengths):
    bounds = jnp.cumsum(doc_lengths, axis=1) - doc_lengths
    before = bounds[:, None, :] <= positions[None, :, None]
    return jnp.max(jnp.where(before, bounds[:, None, :], -1), axis=2)


def tap_mask(positions, starts, spacing):
    return (positions[None, :] - spacing >= starts)[:, :, None]


def shards(tokens, doc_lengths, low_taps, high_taps, level_weights, mix_weight, out_grad):
    batch_size, row_count, channels = tokens.shape
    levels = level_weights.shape[0] - 1
    seq_count = lax.axis_size("seq")
    core_count = lax.axis_size("dp")
    grad_scale = float(batch_size * row_count * seq_count * core_count) ** (-0.5)
    offset = lax.axis_index("seq") * row_count
    positions = offset + jnp.arange(row_count, dtype=jnp.int32)
    starts = doc_starts(positions, doc_lengths)
    shallow = min(levels, row_count.bit_length() - 1)
    summed = jnp.zeros(tokens.shape, jnp.float32)
    states = [tokens]
    previous_list = []
    current = tokens
    for level_index in range(shallow):
        spacing = 2**level_index
        border = shifted_2(current[:, row_count - spacing :, :], "seq", 1)
        shifted = jnp.concatenate([border, current[:, : row_count - spacing, :]], axis=1)
        previous = jnp.where(tap_mask(positions, starts, spacing), shifted, jnp.zeros_like(shifted))
        summed = summed + level_weights[level_index] * (
            high_taps[0] * previous + high_taps[1] * current
        )
        current = (low_taps[0] * previous + low_taps[1] * current).astype(jnp.bfloat16)
        previous_list.append(previous)
        states.append(current)
    for level_index in range(shallow, levels):
        spacing = 2**level_index
        device_hops = spacing // row_count
        if device_hops < seq_count:
            shifted = shifted_2(current, "seq", device_hops)
        else:
            shifted = jnp.zeros_like(current)
        previous = jnp.where(tap_mask(positions, starts, spacing), shifted, jnp.zeros_like(shifted))
        summed = summed + level_weights[level_index] * (
            high_taps[0] * previous + high_taps[1] * current
        )
        current = (low_taps[0] * previous + low_taps[1] * current).astype(jnp.bfloat16)
        previous_list.append(previous)
        states.append(current)
    summed = summed + level_weights[levels] * current
    activated = gelu_value(summed).astype(jnp.bfloat16)
    partial_mix = jnp.einsum(
        "brc,oc->bro", activated, mix_weight, preferred_element_type=jnp.float32
    )
    mixed = lax.psum_scatter(
        partial_mix.astype(jnp.bfloat16), "tensor", scatter_dimension=2, tiled=True
    ).astype(jnp.float32)
    result = (tokens.astype(jnp.float32) + mixed).astype(jnp.bfloat16)
    gathered = lax.all_gather(out_grad, "tensor", axis=2, tiled=True)
    act_grad = jnp.einsum("bro,oc->brc", gathered, mix_weight, preferred_element_type=jnp.float32)
    weight_grad = lax.psum_scatter(
        (
            jnp.einsum("bro,brc->oc", gathered, activated, preferred_element_type=jnp.float32)
            * grad_scale
        ).astype(jnp.bfloat16),
        ("seq", "dp"),
        scatter_dimension=0,
        tiled=True,
    )
    summed_grad = act_grad * gelu_slope(summed)
    carry_grad = (level_weights[levels] * summed_grad).astype(jnp.bfloat16)
    weight_sums = [None] * (levels + 1)
    weight_sums[levels] = jnp.sum(summed_grad * states[levels].astype(jnp.float32), axis=(0, 1))
    low_first = jnp.zeros((channels,), jnp.float32)
    low_second = jnp.zeros((channels,), jnp.float32)
    high_first = jnp.zeros((channels,), jnp.float32)
    high_second = jnp.zeros((channels,), jnp.float32)
    for level_index in range(levels - 1, -1, -1):
        spacing = 2**level_index
        current = states[level_index]
        previous = previous_list[level_index]
        weighted = level_weights[level_index] * summed_grad
        highpass = high_taps[0] * previous + high_taps[1] * current
        weight_sums[level_index] = jnp.sum(summed_grad * highpass, axis=(0, 1))
        grad_wide = carry_grad.astype(jnp.float32)
        low_first = low_first + jnp.sum(grad_wide * previous.astype(jnp.float32), axis=(0, 1))
        low_second = low_second + jnp.sum(grad_wide * current.astype(jnp.float32), axis=(0, 1))
        high_first = high_first + jnp.sum(weighted * previous.astype(jnp.float32), axis=(0, 1))
        high_second = high_second + jnp.sum(weighted * current.astype(jnp.float32), axis=(0, 1))
        carried = low_taps[0] * carry_grad + high_taps[0] * weighted
        stayed = low_taps[1] * carry_grad + high_taps[1] * weighted
        outgoing = jnp.where(
            tap_mask(positions, starts, spacing), carried, jnp.zeros_like(carried)
        ).astype(jnp.bfloat16)
        if level_index < shallow:
            border = shifted_2(outgoing[:, :spacing, :], "seq", -1)
            pulled = jnp.concatenate([outgoing[:, spacing:, :], border], axis=1)
        else:
            device_hops = spacing // row_count
            if device_hops < seq_count:
                pulled = shifted_2(outgoing, "seq", -device_hops)
            else:
                pulled = jnp.zeros_like(outgoing)
        carry_grad = (stayed + pulled).astype(jnp.bfloat16)
    token_grad = (out_grad.astype(jnp.float32) + carry_grad.astype(jnp.float32)).astype(
        jnp.bfloat16
    )
    low_grad = jnp.stack([low_first, low_second]) * grad_scale
    high_grad = jnp.stack([high_first, high_second]) * grad_scale
    level_grad = jnp.stack(weight_sums) * grad_scale
    low_grad, high_grad, level_grad = (
        lax.psum(low_grad.astype(jnp.bfloat16), ("seq", "dp")).astype(jnp.float32),
        lax.psum(high_grad.astype(jnp.bfloat16), ("seq", "dp")).astype(jnp.float32),
        lax.psum(level_grad.astype(jnp.bfloat16), ("seq", "dp")).astype(jnp.float32),
    )
    return (result, token_grad, weight_grad, low_grad, high_grad, level_grad)


def solution(mesh):
    placed = (
        P(("groups", "dp"), "seq", "tensor"),
        P(("groups", "dp"), None),
        P(None, "tensor"),
        P(None, "tensor"),
        P(None, "tensor"),
        P(None, "tensor"),
        P(("groups", "dp"), "seq", "tensor"),
    )
    return jax.shard_map(
        shards,
        mesh=mesh,
        in_specs=placed,
        out_specs=(
            P(("groups", "dp"), "seq", "tensor"),
            P(("groups", "dp"), "seq", "tensor"),
            P(("groups", "seq", "dp"), "tensor"),
            P("groups", "tensor"),
            P("groups", "tensor"),
            P("groups", "tensor"),
        ),
        check_vma=False,
    )
```

profile of v0, /device:TPU:0, one launch (start us, length us, event | category | flops | bytes accessed | tf_op | source)
XLA Modules:
  0.0 565.9 jit_solution(1448448901782919432)
XLA Ops:
  8.0 4.9 collective-permute-start
  16.0 2.2 fusion.18
  18.3 3.5 collective-permute-start.1
  21.8 1.3 collective-permute-done.1
  23.9 4.2 collective-permute-start.2
  28.1 1.4 collective-permute-done.2
  30.2 4.2 collective-permute-start.3
  34.5 1.5 collective-permute-done.3
  36.7 4.2 collective-permute-start.4
  41.0 1.8 collective-permute-done.4
  43.4 4.3 collective-permute-start.5
  47.7 3.5 collective-permute-done.5
  51.8 4.4 collective-permute-start.6
  56.3 6.0 %collective-permute-done.6 = bf16[1,64,2048]{2,1,0:T(8,128)(2,1)S(1)} collective-permute-done((bf16[1,64,2048]{2,1,0:T(8,128)(2,1)S(1)}, bf16[1,64,2048]{2,1,0:T(8,128)(2,1)S(1)}, u32[]{:S(2)}, u32[]{:S(2)}) %collective-permute-start.6) | collective-permute-done | bytes 262176 | tf_op jit(solution)/shard_map/ppermute | solution.py:13
  63.0 4.4 collective-permute-start.7
  67.4 8.8 %collective-permute-done.7 = bf16[1,128,2048]{2,1,0:T(8,128)(2,1)S(1)} collective-permute-done((bf16[1,128,2048]{2,1,0:T(8,128)(2,1)S(1)}, bf16[1,128,2048]{2,1,0:T(8,128)(2,1)S(1)}, u32[]{:S(2)}, u32[]{:S(2)}) %collective-permute-start.7) | collective-permute-done | bytes 524320 | tf_op jit(solution)/shard_map/ppermute | solution.py:13
  76.2 1.5 fusion.52
  77.7 5.5 collective-permute-start.8
  83.5 14.6 %collective-permute-done.8 = bf16[1,256,2048]{2,1,0:T(8,128)(2,1)} collective-permute-done((bf16[1,256,2048]{2,1,0:T(8,128)(2,1)}, bf16[1,256,2048]{2,1,0:T(8,128)(2,1)}, u32[]{:S(2)}, u32[]{:S(2)}) %collective-permute-start.8) | collective-permute-done | bytes 1048608 | tf_op jit(solution)/shard_map/ppermute | solution.py:13
  98.1 2.1 fusion.57
  100.2 17.4 %collective-permute-start.9 = (bf16[1,256,2048]{2,1,0:T(8,128)(2,1)S(1)}, bf16[1,256,2048]{2,1,0:T(8,128)(2,1)S(1)}, u32[]{:S(2)}, u32[]{:S(2)}) collective-permute-start(bf16[1,256,2048]{2,1,0:T(8,128)(2,1)S(1)} %fusion.57), channel_id=1, source_target_pairs={{0,8},{4,12},{1,9},{5,13},{2,10},{6,14},{3,11},{7,15},{16,24},{20,... | collective-permute-start | bytes 3145736 | tf_op jit(solution)/shard_map/ppermute | solution.py:13
  117.5 1.7 fusion.183
  119.4 10.2 %collective-permute-done.9 = bf16[1,256,2048]{2,1,0:T(8,128)(2,1)S(1)} collective-permute-done((bf16[1,256,2048]{2,1,0:T(8,128)(2,1)S(1)}, bf16[1,256,2048]{2,1,0:T(8,128)(2,1)S(1)}, u32[]{:S(2)}, u32[]{:S(2)}) %collective-permute-start.9) | collective-permute-done | bytes 1048608 | tf_op jit(solution)/shard_map/ppermute | solution.py:13
  130.9 13.8 %fusion.3 = (f32[1,256,2048]{2,1,0:T(8,128)}, bf16[1,256,2048]{2,1,0:T(8,128)(2,1)}) fusion(bf16[1,256,2048]{2,1,0:T(8,128)(2,1)S(1)} %fusion.57, bf16[1,256,2048]{2,1,0:T(8,128)(2,1)} %fusion.52, bf16[1,256,2048]{2,1,0:T(8,128)(2,1)} %copy-done.15, bf16[1,256,2048]{2,1,0:T(8,128)(2,1)} %copy-done.13, bf16[1,256,2048]{2,1,0:T(8,128)(2,1)S(1)} %copy-done.11, ...), kind=kLoop, calls=%fused_computation.123 | loop fusion | flops 70254592 | bytes 24275456 | tf_op jit(solution)/shard_map/add | solution.py:77
  144.8 11.1 %fusion.88 = (bf16[1,256,2048]{2,1,0:T(8,128)(2,1)S(1)}, f32[1,256,2048]{2,1,0:T(8,128)S(1)}) fusion(f32[2048]{0:T(1024)} %bitcast.180, f32[2048]{0:T(1024)S(1)} %bitcast.105, f32[2048]{0:T(1024)} %bitcast.133, pred[256]{0:T(512)(128)(4,1)} %get-tuple-element.139, f32[2048]{0:T(1024)} %bitcast.177, f32[2048]{0:T(1024)} %bitcast.186, f32[2048]{0:T(1024)} %bitcast.116, ...), kind=kOutput, calls=%fused_computation.208 | convolution fusion | flops 4315414528 | bytes 24183040 | tf_op jit(solution)/shard_map/bro,oc->brc/dot_general | solution.py:87
  155.9 1.3 collective-permute-start.10
  157.2 38.8 %collective-permute-done.10 = bf16[1,256,2048]{2,1,0:T(8,128)(2,1)S(1)} collective-permute-done((bf16[1,256,2048]{2,1,0:T(8,128)(2,1)S(1)}, bf16[1,256,2048]{2,1,0:T(8,128)(2,1)S(1)}, u32[]{:S(2)}, u32[]{:S(2)}) %collective-permute-start.10) | collective-permute-done | bytes 1048608 | tf_op jit(solution)/shard_map/ppermute | solution.py:13
  196.1 8.5 %fusion.4 = (f32[2048]{0:T(1024)}, f32[2048]{0:T(1024)}, f32[2048]{0:T(1024)}, f32[2048]{0:T(1024)}, f32[2048]{0:T(1024)}, /*index=5*/f32[2048]{0:T(1024)}, f32[...) fusion(f32[1,256,2048]{2,1,0:T(8,128)S(1)} %get-tuple-element.1, ...), kind=kLoop, calls=%fused_computation.124 | loop fusion | flops 47667200 | bytes 9691648 | tf_op jit(solution)/shard_map/reduce_sum | solution.py:100
  205.2 1.3 collective-permute-start.11
  206.5 21.0 %collective-permute-done.11 = bf16[1,256,2048]{2,1,0:T(8,128)(2,1)S(1)} collective-permute-done((bf16[1,256,2048]{2,1,0:T(8,128)(2,1)S(1)}, bf16[1,256,2048]{2,1,0:T(8,128)(2,1)S(1)}, u32[]{:S(2)}, u32[]{:S(2)}) %collective-permute-start.11) | collective-permute-done | bytes 1048608 | tf_op jit(solution)/shard_map/ppermute | solution.py:13
  227.5 1.5 fusion.105
  229.6 1.6 collective-permute-start.12
  231.3 12.4 %collective-permute-done.12 = bf16[1,128,2048]{2,1,0:T(8,128)(2,1)S(1)} collective-permute-done((bf16[1,128,2048]{2,1,0:T(8,128)(2,1)S(1)}, bf16[1,128,2048]{2,1,0:T(8,128)(2,1)S(1)}, u32[]{:S(2)}, u32[]{:S(2)}) %collective-permute-start.12) | collective-permute-done | bytes 524320 | tf_op jit(solution)/shard_map/ppermute | solution.py:13
  243.7 1.5 fusion.113
  245.2 4.6 multiply_reduce_fusion.2
  249.8 1.4 collective-permute-start.13
  251.3 6.9 %collective-permute-done.13 = bf16[1,64,2048]{2,1,0:T(8,128)(2,1)S(1)} collective-permute-done((bf16[1,64,2048]{2,1,0:T(8,128)(2,1)S(1)}, bf16[1,64,2048]{2,1,0:T(8,128)(2,1)S(1)}, u32[]{:S(2)}, u32[]{:S(2)}) %collective-permute-start.13) | collective-permute-done | bytes 262176 | tf_op jit(solution)/shard_map/ppermute | solution.py:13
  258.2 1.5 fusion.121
  263.0 12.5 %fusion.1 = bf16[1,256,4096]{2,1,0:T(8,128)(2,1)} fusion(bf16[4096,2048]{1,0:T(8,128)(2,1)} %param.12, f32[1,256,2048]{2,1,0:T(8,128)} %get-tuple-element.111), kind=kOutput, calls=%fused_computation.3 | convolution fusion | flops 4300734464 | bytes 20971520 | tf_op jit(solution)/shard_map/brc,oc->bro/dot_general | solution.py:79
  275.9 1.3 slice.165
  277.4 2.3 fusion.129
  279.8 3.8 multiply_reduce_fusion.4
  283.6 1.4 collective-permute-start.15
  285.1 5.4 collective-permute-done.15
  292.0 1.3 collective-permute-start.16
  293.4 4.4 collective-permute-done.16
  298.8 4.1 multiply_reduce_fusion.6
  302.9 1.4 collective-permute-start.17
  304.6 4.1 collective-permute-done.17
  310.3 1.6 collective-permute-start.18
  312.2 3.7 collective-permute-done.18
  316.0 2.0 fusion.161
  318.4 7.1 %multiply_reduce_fusion.8 = (f32[2048]{0:T(1024)}, f32[2048]{0:T(1024)}, f32[2048]{0:T(1024)}, f32[2048]{0:T(1024)}, f32[2048]{0:T(1024)}, /*index=5*/f32[2048]{...) fusion(f32[1,256,2048]{2,1,0:T(8,128)S(1)} %get-tuple-element.150, ...), kind=kLoop, calls=%fused_computation.295 | loop fusion | flops 25149440 | bytes 11641344 | tf_op jit(solution)/shard_map/reduce_sum | solution.py:111
  325.6 1.7 stack.67
  331.7 13.1 %fusion = bf16[4096,2048]{0,1:T(8,128)(2,1)} fusion(bf16[1,256,4096]{2,1,0:T(8,128)(2,1)} %all-gather.2.cloned.1.call-done, f32[1,256,2048]{2,1,0:T(8,128)} %get-tuple-element.111), kind=kOutput, calls=%fused_computation.1 | convolution fusion | flops 4316463104 | bytes 20971520 | tf_op jit(solution)/shard_map/bro,brc->oc/dot_general | solution.py:90
  346.0 1.3 collective-permute-start.19
  347.5 4.0 collective-permute-done.19
  351.6 1.7 add_convert_fusion
  353.3 28.3 %all-reduce.3.cloned.1.call-done = (bf16[2,2048]{1,0:T(2,128)(2,1)}, bf16[2,2048]{1,0:T(2,128)(2,1)}, bf16[13,2048]{1,0:T(8,128)(2,1)}) async-done(((bf16[2,2048]{1,0:T(2,128)(2,1)}, bf16[2,2048]{1,0:T(2,128)(2,1)}, bf16[13,2048]{1,0:T(8,128)(2,1)}), (bf16[2,2048]{1,0:T(2,128)(2,1)}, bf16[2,2048]{1,0:T(2,128)(2,1)}, bf16[13,2048]{1,0:T(8,128)(2,1)})) %all-reduce.3.cloned.1.call-update) | async-done | bytes 69648 | tf_op jit(solution)/shard_map/psum | solution.py:139
  381.6 1.3 convert_element_type.712
  382.9 1.3 convert_element_type.714
  384.2 1.5 convert_element_type.716
  385.7 169.5 %reduce-scatter.5.cloned.1.call-done = bf16[512,2048]{0,1:T(8,128)(2,1)} async-done(((bf16[4096,2048]{0,1:T(8,128)(2,1)}), bf16[512,2048]{0,1:T(8,128)(2,1)}) %reduce-scatter.5.cloned.1.call-update) | async-done | bytes 2097168 | tf_op jit(solution)/shard_map/reduce_scatter | solution.py:88
  555.2 3.9 copy.14
  (380 shorter events, 24.7 us)
Async XLA Ops:
  7.2 137.5 %all-gather.2.cloned.1.call-start = ((), (), s32[]{:S(2)}) async-start(), calls=%async_computation.3 | async-start | bytes 3145728 | tf_op jit(solution)/shard_map/all_gather | solution.py:86
  8.0 8.0 %collective-permute-start = (bf16[1,1,2048]{2,1,0:T(2,128)(2,1)S(1)}, bf16[1,1,2048]{2,1,0:T(2,128)(2,1)S(1)}, u32[]{:S(2)}, u32[]{:S(2)}) collective-permute-start(bf16[1,1,2048]{2,1,0:T(2,128)(2,1)S(1)} %slice.100), channel_id=1, source_target_pairs={{0,4},{4,8},{8,12},{1,5},{5,9},{9,13},{2,6},{6,10},{10,14},{3,7},{... | collective-permute-start | bytes 12296 | tf_op jit(solution)/shard_map/ppermute | solution.py:13
  15.9 26.8 %copy-start.143 = (pred[256]{0:T(512)(128)(4,1)}, pred[256]{0:T(512)(128)(4,1)S(1)}, u32[]{:S(2)}) copy-start(pred[256]{0:T(512)(128)(4,1)S(1)} %get-tuple-element.144) | copy-start | bytes 772
  16.0 35.3 %copy-start.129 = (pred[256]{0:T(512)(128)(4,1)}, pred[256]{0:T(512)(128)(4,1)S(1)}, u32[]{:S(2)}) copy-start(pred[256]{0:T(512)(128)(4,1)S(1)} %get-tuple-element.143) | copy-start | bytes 772
  16.0 46.3 %copy-start.146 = (pred[256]{0:T(512)(128)(4,1)}, pred[256]{0:T(512)(128)(4,1)S(1)}, u32[]{:S(2)}) copy-start(pred[256]{0:T(512)(128)(4,1)S(1)} %get-tuple-element.142) | copy-start | bytes 772
  16.0 60.2 %copy-start.133 = (pred[256]{0:T(512)(128)(4,1)}, pred[256]{0:T(512)(128)(4,1)S(1)}, u32[]{:S(2)}) copy-start(pred[256]{0:T(512)(128)(4,1)S(1)} %get-tuple-element.141) | copy-start | bytes 772
  18.3 111.4 %copy-start = (bf16[1,256,2048]{2,1,0:T(8,128)(2,1)}, bf16[1,256,2048]{2,1,0:T(8,128)(2,1)S(1)}, u32[]{:S(2)}) copy-start(bf16[1,256,2048]{2,1,0:T(8,128)(2,1)S(1)} %fusion.18) | copy-start | bytes 3145732
  18.3 4.8 collective-permute-start.1
  23.9 5.6 collective-permute-start.2
  30.2 5.8 %collective-permute-start.3 = (bf16[1,8,2048]{2,1,0:T(8,128)(2,1)S(1)}, bf16[1,8,2048]{2,1,0:T(8,128)(2,1)S(1)}, u32[]{:S(2)}, u32[]{:S(2)}) collective-permute-start(bf16[1,8,2048]{2,1,0:T(8,128)(2,1)S(1)} %slice.151), channel_id=1, source_target_pairs={{0,4},{4,8},{8,12},{1,5},{5,9},{9,13},{2,6},{6,10},{10,14},{3,7},{... | collective-permute-start | bytes 98312 | tf_op jit(solution)/shard_map/ppermute | solution.py:13
  36.7 6.1 %collective-permute-start.4 = (bf16[1,16,2048]{2,1,0:T(8,128)(2,1)S(1)}, bf16[1,16,2048]{2,1,0:T(8,128)(2,1)S(1)}, u32[]{:S(2)}, u32[]{:S(2)}) collective-permute-start(bf16[1,16,2048]{2,1,0:T(8,128)(2,1)S(1)} %slice.153), channel_id=1, source_target_pairs={{0,4},{4,8},{8,12},{1,5},{5,9},{9,13},{2,6},{6,10},{10,14},{3,7},{... | collective-permute-start | bytes 196616 | tf_op jit(solution)/shard_map/ppermute | solution.py:13
  43.4 7.8 %collective-permute-start.5 = (bf16[1,32,2048]{2,1,0:T(8,128)(2,1)S(1)}, bf16[1,32,2048]{2,1,0:T(8,128)(2,1)S(1)}, u32[]{:S(2)}, u32[]{:S(2)}) collective-permute-start(bf16[1,32,2048]{2,1,0:T(8,128)(2,1)S(1)} %slice.155), channel_id=1, source_target_pairs={{0,4},{4,8},{8,12},{1,5},{5,9},{9,13},{2,6},{6,10},{10,14},{3,7},{... | collective-permute-start | bytes 393224 | tf_op jit(solution)/shard_map/ppermute | solution.py:13
  51.8 10.5 %collective-permute-start.6 = (bf16[1,64,2048]{2,1,0:T(8,128)(2,1)S(1)}, bf16[1,64,2048]{2,1,0:T(8,128)(2,1)S(1)}, u32[]{:S(2)}, u32[]{:S(2)}) collective-permute-start(bf16[1,64,2048]{2,1,0:T(8,128)(2,1)S(1)} %slice.157), channel_id=1, source_target_pairs={{0,4},{4,8},{8,12},{1,5},{5,9},{9,13},{2,6},{6,10},{10,14},{3,7},{... | collective-permute-start | bytes 786440 | tf_op jit(solution)/shard_map/ppermute | solution.py:13
  63.0 13.2 %collective-permute-start.7 = (bf16[1,128,2048]{2,1,0:T(8,128)(2,1)S(1)}, bf16[1,128,2048]{2,1,0:T(8,128)(2,1)S(1)}, u32[]{:S(2)}, u32[]{:S(2)}) collective-permute-start(bf16[1,128,2048]{2,1,0:T(8,128)(2,1)S(1)} %get-tuple-element.120), channel_id=1, source_target_pairs={{0,4},{4,8},{8,12},{1,5},{5,9},{9,13},{2,6},{6,10},{10,14},{3,7},{... | collective-permute-start | bytes 1572872 | tf_op jit(solution)/shard_map/ppermute | solution.py:13
  77.7 53.0 %copy-start.2 = (bf16[1,256,2048]{2,1,0:T(8,128)(2,1)S(1)}, bf16[1,256,2048]{2,1,0:T(8,128)(2,1)}, u32[]{:S(2)}) copy-start(bf16[1,256,2048]{2,1,0:T(8,128)(2,1)} %param.7) | copy-start | bytes 3145732
  77.7 20.4 %collective-permute-start.8 = (bf16[1,256,2048]{2,1,0:T(8,128)(2,1)}, bf16[1,256,2048]{2,1,0:T(8,128)(2,1)}, u32[]{:S(2)}, u32[]{:S(2)}) collective-permute-start(bf16[1,256,2048]{2,1,0:T(8,128)(2,1)} %fusion.52), channel_id=1, source_target_pairs={{0,4},{4,8},{8,12},{1,5},{5,9},{9,13},{2,6},{6,10},{10,14},{3,7},{... | collective-permute-start | bytes 3145736 | tf_op jit(solution)/shard_map/ppermute | solution.py:13
  83.2 234.9 %reduce-scatter.3.cloned.1.call-start = ((), (), s32[]{:S(2)}) async-start(), calls=%async_computation.2 | async-start | bytes 3145728 | tf_op jit(solution)/shard_map/reduce_scatter | solution.py:82
  83.3 35.9 %copy-start.139 = (f32[2,2048]{1,0:T(2,128)S(1)}, f32[2,2048]{1,0:T(2,128)}, u32[]{:S(2)}) copy-start(f32[2,2048]{1,0:T(2,128)} %param.10) | copy-start | bytes 49156
  83.3 47.4 %copy-start.5 = (bf16[1,256,2048]{2,1,0:T(8,128)(2,1)S(1)}, bf16[1,256,2048]{2,1,0:T(8,128)(2,1)}, u32[]{:S(2)}) copy-start(bf16[1,256,2048]{2,1,0:T(8,128)(2,1)} %copy-done.4) | copy-start | bytes 3145732
  83.3 47.4 %copy-start.8 = (bf16[1,256,2048]{2,1,0:T(8,128)(2,1)S(1)}, bf16[1,256,2048]{2,1,0:T(8,128)(2,1)}, u32[]{:S(2)}) copy-start(bf16[1,256,2048]{2,1,0:T(8,128)(2,1)} %copy-done.7) | copy-start | bytes 3145732
  83.3 47.4 %copy-start.11 = (bf16[1,256,2048]{2,1,0:T(8,128)(2,1)S(1)}, bf16[1,256,2048]{2,1,0:T(8,128)(2,1)}, u32[]{:S(2)}) copy-start(bf16[1,256,2048]{2,1,0:T(8,128)(2,1)} %copy-done.10) | copy-start | bytes 3145732
  83.3 47.4 %copy-start.49 = (bf16[1,16,2048]{2,1,0:T(8,128)(2,1)S(1)}, bf16[1,16,2048]{2,1,0:T(8,128)(2,1)}, u32[]{:S(2)}) copy-start(bf16[1,16,2048]{2,1,0:T(8,128)(2,1)} %copy-done.48) | copy-start | bytes 196612
  83.3 47.4 %copy-start.52 = (bf16[1,8,2048]{2,1,0:T(8,128)(2,1)S(1)}, bf16[1,8,2048]{2,1,0:T(8,128)(2,1)}, u32[]{:S(2)}) copy-start(bf16[1,8,2048]{2,1,0:T(8,128)(2,1)} %copy-done.51) | copy-start | bytes 98308
  83.4 47.4 %copy-start.55 = (bf16[1,4,2048]{2,1,0:T(4,128)(2,1)S(1)}, bf16[1,4,2048]{2,1,0:T(4,128)(2,1)}, u32[]{:S(2)}) copy-start(bf16[1,4,2048]{2,1,0:T(4,128)(2,1)} %copy-done.54) | copy-start | bytes 49156
  83.4 47.4 %copy-start.69 = (bf16[1,1,2048]{2,1,0:T(2,128)(2,1)S(1)}, bf16[1,1,2048]{2,1,0:T(2,128)(2,1)}, u32[]{:S(2)}) copy-start(bf16[1,1,2048]{2,1,0:T(2,128)(2,1)} %copy-done.68) | copy-start | bytes 12292
  83.4 47.4 %copy-start.72 = (bf16[1,2,2048]{2,1,0:T(2,128)(2,1)S(1)}, bf16[1,2,2048]{2,1,0:T(2,128)(2,1)}, u32[]{:S(2)}) copy-start(bf16[1,2,2048]{2,1,0:T(2,128)(2,1)} %copy-done.71) | copy-start | bytes 24580
  83.4 47.4 %copy-start.127 = (pred[256]{0:T(512)(128)(4,1)S(1)}, pred[256]{0:T(512)(128)(4,1)}, u32[]{:S(2)}) copy-start(pred[256]{0:T(512)(128)(4,1)} %copy-done.126) | copy-start | bytes 772
  83.4 47.4 %copy-start.130 = (pred[256]{0:T(512)(128)(4,1)S(1)}, pred[256]{0:T(512)(128)(4,1)}, u32[]{:S(2)}) copy-start(pred[256]{0:T(512)(128)(4,1)} %copy-done.129) | copy-start | bytes 772
  83.4 47.4 %copy-start.134 = (pred[256]{0:T(512)(128)(4,1)S(1)}, pred[256]{0:T(512)(128)(4,1)}, u32[]{:S(2)}) copy-start(pred[256]{0:T(512)(128)(4,1)} %copy-done.133) | copy-start | bytes 772
  83.4 47.4 %copy-start.137 = (pred[256]{0:T(512)(128)(4,1)S(1)}, pred[256]{0:T(512)(128)(4,1)}, u32[]{:S(2)}) copy-start(pred[256]{0:T(512)(128)(4,1)} %copy-done.136) | copy-start | bytes 772
  83.4 47.4 %copy-start.141 = (pred[256]{0:T(512)(128)(4,1)S(1)}, pred[256]{0:T(512)(128)(4,1)}, u32[]{:S(2)}) copy-start(pred[256]{0:T(512)(128)(4,1)} %copy-done.140) | copy-start | bytes 772
  83.4 47.4 %copy-start.144 = (pred[256]{0:T(512)(128)(4,1)S(1)}, pred[256]{0:T(512)(128)(4,1)}, u32[]{:S(2)}) copy-start(pred[256]{0:T(512)(128)(4,1)} %copy-done.143) | copy-start | bytes 772
  83.4 47.4 %copy-start.147 = (pred[256]{0:T(512)(128)(4,1)S(1)}, pred[256]{0:T(512)(128)(4,1)}, u32[]{:S(2)}) copy-start(pred[256]{0:T(512)(128)(4,1)} %copy-done.146) | copy-start | bytes 772
  83.5 47.4 %copy-start.149 = (pred[256]{0:T(512)(128)(4,1)S(1)}, pred[256]{0:T(512)(128)(4,1)}, u32[]{:S(2)}) copy-start(pred[256]{0:T(512)(128)(4,1)} %get-tuple-element.140) | copy-start | bytes 772
  83.5 47.4 %copy-start.152 = (pred[256]{0:T(512)(128)(4,1)S(1)}, pred[256]{0:T(512)(128)(4,1)}, u32[]{:S(2)}) copy-start(pred[256]{0:T(512)(128)(4,1)} %copy-done.151) | copy-start | bytes 772
  83.5 47.4 %copy-start.154 = (pred[256]{0:T(512)(128)(4,1)S(1)}, pred[256]{0:T(512)(128)(4,1)}, u32[]{:S(2)}) copy-start(pred[256]{0:T(512)(128)(4,1)} %get-tuple-element.139) | copy-start | bytes 772
  100.2 29.5 %copy-start.31 = (bf16[1,256,2048]{2,1,0:T(8,128)(2,1)}, bf16[1,256,2048]{2,1,0:T(8,128)(2,1)S(1)}, u32[]{:S(2)}) copy-start(bf16[1,256,2048]{2,1,0:T(8,128)(2,1)S(1)} %fusion.57) | copy-start | bytes 3145732
  100.2 29.5 %collective-permute-start.9 = (bf16[1,256,2048]{2,1,0:T(8,128)(2,1)S(1)}, bf16[1,256,2048]{2,1,0:T(8,128)(2,1)S(1)}, u32[]{:S(2)}, u32[]{:S(2)}) collective-permute-start(bf16[1,256,2048]{2,1,0:T(8,128)(2,1)S(1)} %fusion.57), channel_id=1, source_target_pairs={{0,8},{4,12},{1,9},{5,13},{2,10},{6,14},{3,11},{7,15},{16,24},{20,... | collective-permute-start | bytes 3145736 | tf_op jit(solution)/shard_map/ppermute | solution.py:13
  144.6 51.4 %copy-start.32 = (bf16[1,256,2048]{2,1,0:T(8,128)(2,1)S(1)}, bf16[1,256,2048]{2,1,0:T(8,128)(2,1)}, u32[]{:S(2)}) copy-start(bf16[1,256,2048]{2,1,0:T(8,128)(2,1)} %copy-done.31) | copy-start | bytes 3145732
  144.7 51.4 %copy-start.38 = (bf16[1,256,2048]{2,1,0:T(8,128)(2,1)S(1)}, bf16[1,256,2048]{2,1,0:T(8,128)(2,1)}, u32[]{:S(2)}) copy-start(bf16[1,256,2048]{2,1,0:T(8,128)(2,1)} %copy-done.37) | copy-start | bytes 3145732
  144.7 51.4 %copy-start.39 = (bf16[1,256,2048]{2,1,0:T(8,128)(2,1)S(1)}, bf16[1,256,2048]{2,1,0:T(8,128)(2,1)}, u32[]{:S(2)}) copy-start(bf16[1,256,2048]{2,1,0:T(8,128)(2,1)} %get-tuple-element.112) | copy-start | bytes 3145732
  144.7 51.3 %copy-start.43 = (f32[1,2048]{1,0:T(1,128)S(1)}, f32[1,2048]{1,0:T(1,128)}, u32[]{:S(2)}) copy-start(f32[1,2048]{1,0:T(1,128)} %copy-done.42) | copy-start | bytes 24580
  144.7 51.3 %copy-start.46 = (f32[1,2048]{1,0:T(1,128)S(1)}, f32[1,2048]{1,0:T(1,128)}, u32[]{:S(2)}) copy-start(f32[1,2048]{1,0:T(1,128)} %copy-done.45) | copy-start | bytes 24580
  144.7 51.3 %copy-start.67 = (f32[1,2048]{1,0:T(1,128)S(1)}, f32[1,2048]{1,0:T(1,128)}, u32[]{:S(2)}) copy-start(f32[1,2048]{1,0:T(1,128)} %copy-done.66) | copy-start | bytes 24580
  144.7 51.3 %copy-start.83 = (f32[2048]{0:T(1024)S(1)}, f32[2048]{0:T(1024)}, u32[]{:S(2)}) copy-start(f32[2048]{0:T(1024)} %copy-done.82) | copy-start | bytes 24580
  144.7 51.3 %copy-start.85 = (f32[2048]{0:T(1024)S(1)}, f32[2048]{0:T(1024)}, u32[]{:S(2)}) copy-start(f32[2048]{0:T(1024)} %copy-done.84) | copy-start | bytes 24580
  144.7 51.3 %copy-start.87 = (f32[1,2048]{1,0:T(1,128)S(1)}, f32[1,2048]{1,0:T(1,128)}, u32[]{:S(2)}) copy-start(f32[1,2048]{1,0:T(1,128)} %copy-done.86) | copy-start | bytes 24580
  144.7 51.3 %copy-start.89 = (f32[1,2048]{1,0:T(1,128)S(1)}, f32[1,2048]{1,0:T(1,128)}, u32[]{:S(2)}) copy-start(f32[1,2048]{1,0:T(1,128)} %copy-done.88) | copy-start | bytes 24580
  144.8 51.3 %copy-start.91 = (f32[1,2048]{1,0:T(1,128)S(1)}, f32[1,2048]{1,0:T(1,128)}, u32[]{:S(2)}) copy-start(f32[1,2048]{1,0:T(1,128)} %copy-done.90) | copy-start | bytes 24580
  144.8 51.3 %copy-start.93 = (f32[1,2048]{1,0:T(1,128)S(1)}, f32[1,2048]{1,0:T(1,128)}, u32[]{:S(2)}) copy-start(f32[1,2048]{1,0:T(1,128)} %copy-done.92) | copy-start | bytes 24580
  144.8 51.3 %copy-start.150 = (pred[256]{0:T(512)(128)(4,1)S(1)}, pred[256]{0:T(512)(128)(4,1)}, u32[]{:S(2)}) copy-start(pred[256]{0:T(512)(128)(4,1)} %get-tuple-element.140) | copy-start | bytes 772
  144.8 51.3 %copy-start.155 = (pred[256]{0:T(512)(128)(4,1)S(1)}, pred[256]{0:T(512)(128)(4,1)}, u32[]{:S(2)}) copy-start(pred[256]{0:T(512)(128)(4,1)} %get-tuple-element.139) | copy-start | bytes 772
  155.9 40.1 %collective-permute-start.10 = (bf16[1,256,2048]{2,1,0:T(8,128)(2,1)S(1)}, bf16[1,256,2048]{2,1,0:T(8,128)(2,1)S(1)}, u32[]{:S(2)}, u32[]{:S(2)}) collective-permute-start(bf16[1,256,2048]{2,1,0:T(8,128)(2,1)S(1)} %get-tuple-element.149), channel_id=1, source_target_pairs={{8,0},{12,4},{9,1},{13,5},{10,2},{14,6},{11,3},{15,7},{24,16},{28,... | collective-permute-start | bytes 3145736 | tf_op jit(solution)/shard_map/ppermute | solution.py:13
  205.2 22.3 %collective-permute-start.11 = (bf16[1,256,2048]{2,1,0:T(8,128)(2,1)S(1)}, bf16[1,256,2048]{2,1,0:T(8,128)(2,1)S(1)}, u32[]{:S(2)}, u32[]{:S(2)}) collective-permute-start(bf16[1,256,2048]{2,1,0:T(8,128)(2,1)S(1)} %fusion.96), channel_id=1, source_target_pairs={{4,0},{8,4},{12,8},{5,1},{9,5},{13,9},{6,2},{10,6},{14,10},{7,3},{... | collective-permute-start | bytes 3145736 | tf_op jit(solution)/shard_map/ppermute | solution.py:13
  229.6 14.0 %collective-permute-start.12 = (bf16[1,128,2048]{2,1,0:T(8,128)(2,1)S(1)}, bf16[1,128,2048]{2,1,0:T(8,128)(2,1)S(1)}, u32[]{:S(2)}, u32[]{:S(2)}) collective-permute-start(bf16[1,128,2048]{2,1,0:T(8,128)(2,1)S(1)} %get-tuple-element.119), channel_id=1, source_target_pairs={{4,0},{8,4},{12,8},{5,1},{9,5},{13,9},{6,2},{10,6},{14,10},{7,3},{... | collective-permute-start | bytes 1572872 | tf_op jit(solution)/shard_map/ppermute | solution.py:13
  249.8 8.4 %collective-permute-start.13 = (bf16[1,64,2048]{2,1,0:T(8,128)(2,1)S(1)}, bf16[1,64,2048]{2,1,0:T(8,128)(2,1)S(1)}, u32[]{:S(2)}, u32[]{:S(2)}) collective-permute-start(bf16[1,64,2048]{2,1,0:T(8,128)(2,1)S(1)} %slice.164), channel_id=1, source_target_pairs={{4,0},{8,4},{12,8},{5,1},{9,5},{13,9},{6,2},{10,6},{14,10},{7,3},{... | collective-permute-start | bytes 786440 | tf_op jit(solution)/shard_map/ppermute | solution.py:13
  261.7 15.7 %collective-permute-start.14 = (bf16[1,32,2048]{2,1,0:T(8,128)(2,1)}, bf16[1,32,2048]{2,1,0:T(8,128)(2,1)S(1)}, u32[]{:S(2)}, u32[]{:S(2)}) collective-permute-start(bf16[1,32,2048]{2,1,0:T(8,128)(2,1)} %slice.166), channel_id=1, source_target_pairs={{4,0},{8,4},{12,8},{5,1},{9,5},{13,9},{6,2},{10,6},{14,10},{7,3},{... | collective-permute-start | bytes 393224 | tf_op jit(solution)/shard_map/ppermute | solution.py:13
  275.5 106.1 %all-reduce.3.cloned.1.call-start = ((), (), s32[]{:S(2)}) async-start(), calls=%async_computation.5 | async-start | bytes 163840 | tf_op jit(solution)/shard_map/psum | solution.py:139
  283.6 6.9 %collective-permute-start.15 = (bf16[1,16,2048]{2,1,0:T(8,128)(2,1)S(1)}, bf16[1,16,2048]{2,1,0:T(8,128)(2,1)S(1)}, u32[]{:S(2)}, u32[]{:S(2)}) collective-permute-start(bf16[1,16,2048]{2,1,0:T(8,128)(2,1)S(1)} %slice.168), channel_id=1, source_target_pairs={{4,0},{8,4},{12,8},{5,1},{9,5},{13,9},{6,2},{10,6},{14,10},{7,3},{... | collective-permute-start | bytes 196616 | tf_op jit(solution)/shard_map/ppermute | solution.py:13
  292.0 5.8 %collective-permute-start.16 = (bf16[1,8,2048]{2,1,0:T(8,128)(2,1)S(1)}, bf16[1,8,2048]{2,1,0:T(8,128)(2,1)S(1)}, u32[]{:S(2)}, u32[]{:S(2)}) collective-permute-start(bf16[1,8,2048]{2,1,0:T(8,128)(2,1)S(1)} %slice.170), channel_id=1, source_target_pairs={{4,0},{8,4},{12,8},{5,1},{9,5},{13,9},{6,2},{10,6},{14,10},{7,3},{... | collective-permute-start | bytes 98312 | tf_op jit(solution)/shard_map/ppermute | solution.py:13
  302.9 5.8 %collective-permute-start.17 = (bf16[1,4,2048]{2,1,0:T(4,128)(2,1)S(1)}, bf16[1,4,2048]{2,1,0:T(4,128)(2,1)S(1)}, u32[]{:S(2)}, u32[]{:S(2)}) collective-permute-start(bf16[1,4,2048]{2,1,0:T(4,128)(2,1)S(1)} %slice.172), channel_id=1, source_target_pairs={{4,0},{8,4},{12,8},{5,1},{9,5},{13,9},{6,2},{10,6},{14,10},{7,3},{... | collective-permute-start | bytes 49160 | tf_op jit(solution)/shard_map/ppermute | solution.py:13
  310.3 5.7 %collective-permute-start.18 = (bf16[1,2,2048]{2,1,0:T(2,128)(2,1)S(1)}, bf16[1,2,2048]{2,1,0:T(2,128)(2,1)S(1)}, u32[]{:S(2)}, u32[]{:S(2)}) collective-permute-start(bf16[1,2,2048]{2,1,0:T(2,128)(2,1)S(1)} %slice.348), channel_id=1, source_target_pairs={{4,0},{8,4},{12,8},{5,1},{9,5},{13,9},{6,2},{10,6},{14,10},{7,3},{... | collective-permute-start | bytes 24584 | tf_op jit(solution)/shard_map/ppermute | solution.py:13
  331.6 223.6 %reduce-scatter.5.cloned.1.call-start = ((), (), s32[]{:S(2)}) async-start(), calls=%async_computation.4 | async-start | bytes 18874368 | tf_op jit(solution)/shard_map/reduce_scatter | solution.py:88
  346.0 5.6 collective-permute-start.19
  (116 other events, 937.8 us)
Sparse Core Ops, SparseCore 0:
  83.4 32.4 all-gather.1
  275.6 32.0 reduce-scatter.2
  331.7 49.8 all-reduce.2
  383.8 171.3 reduce-scatter.4
where the time goes:
time: 573 us; the launch traced here: 566 us
  waiting for transfers between devices  348 us (61%)
  other arithmetic  77.7 us (14%)
  starting transfers between devices  71.5 us (12%)
  matrix products  36.7 us (6%)
  between operations  16.3 us (3%)
  local copies, waits for them, and re-layouts  16.1 us (3%)
    reduce_scatter x1, waiting for transfers between devices, shards(): lax.psum_scatter((jnp.einsum('bro,brc->oc', gathered, activated, preferre...  170 us
    ppermute x20, waiting for transfers between devices, shifted_2(): return lax.ppermute(block, axis, route)  150 us
    ppermute x20, starting transfers between devices, shifted_2(): return lax.ppermute(block, axis, route)  70.9 us
    psum x1, waiting for transfers between devices, shards(): lax.psum(low_grad.astype(jnp.bfloat16), ('seq', 'dp')).astype(jnp.float32)  28.3 us
    reduce_sum x4, other arithmetic, shards(): weight_sums[level_index] = jnp.sum(summed_grad * highpass, axis=(0, 1))  19.5 us
    add x1, other arithmetic, shards(): summed = summed + level_weights[levels] * current  13.8 us
    dot_general x1, matrix products, shards(): jnp.einsum('bro,brc->oc', gathered, activated, preferred_element_type=jnp...  13.1 us
    dot_general x1, matrix products, shards(): jnp.einsum('brc,oc->bro', activated, mix_weight, preferred_element_type=j...  12.5 us
  transfers between devices with their start and end apart: 24, of which 20 were waited for; matrix products, arithmetic and copies ran while one was open for 12% of the time, Pallas kernels for 0%

commit v1 on v0

--- a/solution.py
+++ b/solution.py
@@ -136,7 +136,7 @@
     high_grad = jnp.stack([high_first, high_second]) * grad_scale
     level_grad = jnp.stack(weight_sums) * grad_scale
     low_grad, high_grad, level_grad = (
-        lax.psum(low_grad.astype(jnp.bfloat16), ("seq", "dp")).astype(jnp.float32),
+        lax.psum(lax.psum(low_grad.astype(jnp.bfloat16), "dp"), "seq").astype(jnp.float32),
         lax.psum(high_grad.astype(jnp.bfloat16), ("seq", "dp")).astype(jnp.float32),
         lax.psum(level_grad.astype(jnp.bfloat16), ("seq", "dp")).astype(jnp.float32),
     )

time: 573 us -> 478 us (0.83)
  waiting for transfers between devices: 348 us -> 221 us
  blocking collectives: 0 us -> 40.5 us
  other arithmetic: 77.7 us -> 70.5 us
    reduce_scatter x1, waiting for transfers between devices: 170 us -> 0.01 us  [shards(): lax.psum_scatter((jnp.einsum('bro,brc->oc', gathered, activated, preferre...]
    ppermute x20, waiting for transfers between devices: 150 us -> 221 us  [shifted_2(): return lax.ppermute(block, axis, route)]
    psum x0 -> x3, blocking collectives: none -> 40.5 us  [the longest x1 26.9 us: shards(): lax.psum(high_grad.astype(jnp.bfloat16), ('seq', 'dp')).astype(jnp.float32)]
    psum x1 -> x0, waiting for transfers between devices: 28.3 us -> none  [shards(): lax.psum(low_grad.astype(jnp.bfloat16), ('seq', 'dp')).astype(jnp.float32)]
  transfers between devices with their start and end apart: 24 -> 23, of which waited for: 20 -> 18; matrix products, arithmetic and copies ran while one was open for 12% -> 22% of each run, Pallas kernels for 0% -> 0%
where the time goes in v1:
time: 478 us; the launch traced here: 471 us
  waiting for transfers between devices  221 us (46%)
  starting transfers between devices  71.8 us (15%)
  other arithmetic  70.5 us (15%)
  blocking collectives  40.5 us (8%)
  matrix products  33.6 us (7%)
  local copies, waits for them, and re-layouts  16.8 us (4%)
  between operations  16.5 us (3%)
    ppermute x20, waiting for transfers between devices, shifted_2(): return lax.ppermute(block, axis, route)  221 us
    ppermute x20, starting transfers between devices, shifted_2(): return lax.ppermute(block, axis, route)  71.5 us
    psum x1, blocking collectives, shards(): lax.psum(high_grad.astype(jnp.bfloat16), ('seq', 'dp')).astype(jnp.float32)  26.9 us
    reduce_sum x4, other arithmetic, shards(): weight_sums[level_index] = jnp.sum(summed_grad * highpass, axis=(0, 1))  19.5 us
    add x1, other arithmetic, shards(): summed = summed + level_weights[levels] * current  13.8 us
    dot_general x1, matrix products, shards(): jnp.einsum('brc,oc->bro', activated, mix_weight, preferred_element_type=j...  12.4 us
    psum x1, blocking collectives, shards(): lax.psum(lax.psum(low_grad.astype(jnp.bfloat16), 'dp'), 'seq')  11.2 us
    dot_general x1, matrix products, shards(): jnp.einsum('bro,oc->brc', gathered, mix_weight, preferred_element_type=jn...  11.1 us
  transfers between devices with their start and end apart: 23, of which 18 were waited for; matrix products, arithmetic and copies ran while one was open for 22% of the time, Pallas kernels for 0%

profile of v1, /device:TPU:0, one launch (start us, length us, event | category | flops | bytes accessed | tf_op | source)
XLA Modules:
  0.0 470.9 jit_solution(536237196419519168)
XLA Ops:
  8.0 4.9 %collective-permute-start = (bf16[1,1,2048]{2,1,0:T(2,128)(2,1)S(1)}, bf16[1,1,2048]{2,1,0:T(2,128)(2,1)S(1)}, u32[]{:S(2)}, u32[]{:S(2)}) collective-permute-start(bf16[1,1,2048]{2,1,0:T(2,128)(2,1)S(1)} %slice.100), channel_id=1, source_target_pairs={{0,4},{4,8},{8,12},{1,5},{5,9},{9,13},{2,6},{6,10},{10,14},{3,7},{... | collective-permute-start | bytes 12296 | tf_op jit(solution)/shard_map/ppermute | solution.py:13
  16.0 2.3 fusion.18
  18.3 3.5 collective-permute-start.1
  21.8 1.3 collective-permute-done.1
  23.9 4.2 collective-permute-start.2
  28.1 1.4 collective-permute-done.2
  30.3 4.2 collective-permute-start.3
  34.6 1.5 collective-permute-done.3
  36.7 4.2 collective-permute-start.4
  41.0 1.8 collective-permute-done.4
  43.4 4.3 collective-permute-start.5
  47.8 3.5 collective-permute-done.5
  51.8 4.4 collective-permute-start.6
  56.3 6.0 %collective-permute-done.6 = bf16[1,64,2048]{2,1,0:T(8,128)(2,1)S(1)} collective-permute-done((bf16[1,64,2048]{2,1,0:T(8,128)(2,1)S(1)}, bf16[1,64,2048]{2,1,0:T(8,128)(2,1)S(1)}, u32[]{:S(2)}, u32[]{:S(2)}) %collective-permute-start.6) | collective-permute-done | bytes 262176 | tf_op jit(solution)/shard_map/ppermute | solution.py:13
  63.0 4.4 collective-permute-start.7
  67.4 8.8 %collective-permute-done.7 = bf16[1,128,2048]{2,1,0:T(8,128)(2,1)S(1)} collective-permute-done((bf16[1,128,2048]{2,1,0:T(8,128)(2,1)S(1)}, bf16[1,128,2048]{2,1,0:T(8,128)(2,1)S(1)}, u32[]{:S(2)}, u32[]{:S(2)}) %collective-permute-start.7) | collective-permute-done | bytes 524320 | tf_op jit(solution)/shard_map/ppermute | solution.py:13
  76.2 1.5 fusion.52
  77.7 5.6 %collective-permute-start.8 = (bf16[1,256,2048]{2,1,0:T(8,128)(2,1)}, bf16[1,256,2048]{2,1,0:T(8,128)(2,1)}, u32[]{:S(2)}, u32[]{:S(2)}) collective-permute-start(bf16[1,256,2048]{2,1,0:T(8,128)(2,1)} %fusion.52), channel_id=1, source_target_pairs={{0,4},{4,8},{8,12},{1,5},{5,9},{9,13},{2,6},{6,10},{10,14},{3,7},{... | collective-permute-start | bytes 3145736 | tf_op jit(solution)/shard_map/ppermute | solution.py:13
  83.5 14.5 %collective-permute-done.8 = bf16[1,256,2048]{2,1,0:T(8,128)(2,1)} collective-permute-done((bf16[1,256,2048]{2,1,0:T(8,128)(2,1)}, bf16[1,256,2048]{2,1,0:T(8,128)(2,1)}, u32[]{:S(2)}, u32[]{:S(2)}) %collective-permute-start.8) | collective-permute-done | bytes 1048608 | tf_op jit(solution)/shard_map/ppermute | solution.py:13
  98.1 2.1 fusion.57
  100.2 17.7 %collective-permute-start.9 = (bf16[1,256,2048]{2,1,0:T(8,128)(2,1)S(1)}, bf16[1,256,2048]{2,1,0:T(8,128)(2,1)S(1)}, u32[]{:S(2)}, u32[]{:S(2)}) collective-permute-start(bf16[1,256,2048]{2,1,0:T(8,128)(2,1)S(1)} %fusion.57), channel_id=1, source_target_pairs={{0,8},{4,12},{1,9},{5,13},{2,10},{6,14},{3,11},{7,15},{16,24},{20,... | collective-permute-start | bytes 3145736 | tf_op jit(solution)/shard_map/ppermute | solution.py:13
  118.7 1.7 fusion.183
  120.6 9.1 %collective-permute-done.9 = bf16[1,256,2048]{2,1,0:T(8,128)(2,1)S(1)} collective-permute-done((bf16[1,256,2048]{2,1,0:T(8,128)(2,1)S(1)}, bf16[1,256,2048]{2,1,0:T(8,128)(2,1)S(1)}, u32[]{:S(2)}, u32[]{:S(2)}) %collective-permute-start.9) | collective-permute-done | bytes 1048608 | tf_op jit(solution)/shard_map/ppermute | solution.py:13
  129.9 13.8 %fusion.3 = (f32[1,256,2048]{2,1,0:T(8,128)}, bf16[1,256,2048]{2,1,0:T(8,128)(2,1)}) fusion(bf16[1,256,2048]{2,1,0:T(8,128)(2,1)S(1)} %fusion.57, bf16[1,256,2048]{2,1,0:T(8,128)(2,1)} %fusion.52, bf16[1,256,2048]{2,1,0:T(8,128)(2,1)} %copy-done.15, bf16[1,256,2048]{2,1,0:T(8,128)(2,1)} %copy-done.13, bf16[1,256,2048]{2,1,0:T(8,128)(2,1)S(1)} %copy-done.11, ...), kind=kLoop, calls=%fused_computation.123 | loop fusion | flops 70254592 | bytes 24275456 | tf_op jit(solution)/shard_map/add | solution.py:77
  143.8 12.4 %fusion.1 = bf16[1,256,4096]{2,1,0:T(8,128)(2,1)} fusion(bf16[4096,2048]{1,0:T(8,128)(2,1)} %param.12, f32[1,256,2048]{2,1,0:T(8,128)} %get-tuple-element.110), kind=kOutput, calls=%fused_computation.3 | convolution fusion | flops 4300734464 | bytes 20971520 | tf_op jit(solution)/shard_map/brc,oc->bro/dot_general | solution.py:79
  156.5 1.3 copy-done.38
  157.9 10.0 %fusion = bf16[4096,2048]{0,1:T(8,128)(2,1)} fusion(bf16[1,256,4096]{2,1,0:T(8,128)(2,1)} %all-gather.2.cloned.1.call-done, f32[1,256,2048]{2,1,0:T(8,128)S(1)} %copy-done.38), kind=kOutput, calls=%fused_computation.1 | convolution fusion | flops 4316463104 | bytes 20971520 | tf_op jit(solution)/shard_map/bro,brc->oc/dot_general | solution.py:90
  168.1 11.1 %fusion.88 = (bf16[1,256,2048]{2,1,0:T(8,128)(2,1)S(1)}, f32[1,256,2048]{2,1,0:T(8,128)S(1)}) fusion(f32[2048]{0:T(1024)} %bitcast.180, f32[2048]{0:T(1024)S(1)} %bitcast.105, f32[2048]{0:T(1024)} %bitcast.133, pred[256]{0:T(512)(128)(4,1)} %get-tuple-element.138, f32[2048]{0:T(1024)} %bitcast.177, f32[2048]{0:T(1024)} %bitcast.186, f32[2048]{0:T(1024)} %bitcast.116, ...), kind=kOutput, calls=%fused_computation.208 | convolution fusion | flops 4315414528 | bytes 24183040 | tf_op jit(solution)/shard_map/bro,oc->brc/dot_general | solution.py:87
  179.2 1.3 collective-permute-start.10
  180.5 54.0 %collective-permute-done.10 = bf16[1,256,2048]{2,1,0:T(8,128)(2,1)S(1)} collective-permute-done((bf16[1,256,2048]{2,1,0:T(8,128)(2,1)S(1)}, bf16[1,256,2048]{2,1,0:T(8,128)(2,1)S(1)}, u32[]{:S(2)}, u32[]{:S(2)}) %collective-permute-start.10) | collective-permute-done | bytes 1048608 | tf_op jit(solution)/shard_map/ppermute | solution.py:13
  234.6 8.5 %fusion.4 = (f32[2048]{0:T(1024)}, f32[2048]{0:T(1024)}, f32[2048]{0:T(1024)}, f32[2048]{0:T(1024)}, f32[2048]{0:T(1024)}, /*index=5*/f32[2048]{0:T(1024)}, f32[...) fusion(f32[1,256,2048]{2,1,0:T(8,128)S(1)} %get-tuple-element.1, ...), kind=kLoop, calls=%fused_computation.124 | loop fusion | flops 47667200 | bytes 9691648 | tf_op jit(solution)/shard_map/reduce_sum | solution.py:100
  243.6 1.3 collective-permute-start.11
  244.9 49.0 %collective-permute-done.11 = bf16[1,256,2048]{2,1,0:T(8,128)(2,1)S(1)} collective-permute-done((bf16[1,256,2048]{2,1,0:T(8,128)(2,1)S(1)}, bf16[1,256,2048]{2,1,0:T(8,128)(2,1)S(1)}, u32[]{:S(2)}, u32[]{:S(2)}) %collective-permute-start.11) | collective-permute-done | bytes 1048608 | tf_op jit(solution)/shard_map/ppermute | solution.py:13
  295.5 1.6 collective-permute-start.12
  297.1 25.1 %collective-permute-done.12 = bf16[1,128,2048]{2,1,0:T(8,128)(2,1)S(1)} collective-permute-done((bf16[1,128,2048]{2,1,0:T(8,128)(2,1)S(1)}, bf16[1,128,2048]{2,1,0:T(8,128)(2,1)S(1)}, u32[]{:S(2)}, u32[]{:S(2)}) %collective-permute-start.12) | collective-permute-done | bytes 524320 | tf_op jit(solution)/shard_map/ppermute | solution.py:13
  322.2 0.9 fusion.113
  323.8 4.5 multiply_reduce_fusion.2
  328.3 1.4 collective-permute-start.13
  329.9 14.5 %collective-permute-done.13 = bf16[1,64,2048]{2,1,0:T(8,128)(2,1)S(1)} collective-permute-done((bf16[1,64,2048]{2,1,0:T(8,128)(2,1)S(1)}, bf16[1,64,2048]{2,1,0:T(8,128)(2,1)S(1)}, u32[]{:S(2)}, u32[]{:S(2)}) %collective-permute-start.13) | collective-permute-done | bytes 262176 | tf_op jit(solution)/shard_map/ppermute | solution.py:13
  345.9 1.4 collective-permute-start.14
  347.4 9.2 %collective-permute-done.14 = bf16[1,32,2048]{2,1,0:T(8,128)(2,1)S(1)} collective-permute-done((bf16[1,32,2048]{2,1,0:T(8,128)(2,1)S(1)}, bf16[1,32,2048]{2,1,0:T(8,128)(2,1)S(1)}, u32[]{:S(2)}, u32[]{:S(2)}) %collective-permute-start.14) | collective-permute-done | bytes 131104 | tf_op jit(solution)/shard_map/ppermute | solution.py:13
  357.6 3.8 multiply_reduce_fusion.4
  361.4 1.4 collective-permute-start.15
  362.9 6.9 %collective-permute-done.15 = bf16[1,16,2048]{2,1,0:T(8,128)(2,1)S(1)} collective-permute-done((bf16[1,16,2048]{2,1,0:T(8,128)(2,1)S(1)}, bf16[1,16,2048]{2,1,0:T(8,128)(2,1)S(1)}, u32[]{:S(2)}, u32[]{:S(2)}) %collective-permute-start.15) | collective-permute-done | bytes 65568 | tf_op jit(solution)/shard_map/ppermute | solution.py:13
  371.3 1.5 collective-permute-start.16
  372.9 5.4 %collective-permute-done.16 = bf16[1,8,2048]{2,1,0:T(8,128)(2,1)S(1)} collective-permute-done((bf16[1,8,2048]{2,1,0:T(8,128)(2,1)S(1)}, bf16[1,8,2048]{2,1,0:T(8,128)(2,1)S(1)}, u32[]{:S(2)}, u32[]{:S(2)}) %collective-permute-start.16) | collective-permute-done | bytes 32800 | tf_op jit(solution)/shard_map/ppermute | solution.py:13
  378.3 1.0 fusion.145
  379.3 4.1 multiply_reduce_fusion.6
  383.4 1.4 collective-permute-start.17
  385.1 4.8 %collective-permute-done.17 = bf16[1,4,2048]{2,1,0:T(4,128)(2,1)S(1)} collective-permute-done((bf16[1,4,2048]{2,1,0:T(4,128)(2,1)S(1)}, bf16[1,4,2048]{2,1,0:T(4,128)(2,1)S(1)}, u32[]{:S(2)}, u32[]{:S(2)}) %collective-permute-start.17) | collective-permute-done | bytes 16416 | tf_op jit(solution)/shard_map/ppermute | solution.py:13
  389.9 1.1 fusion.153
  391.5 1.4 collective-permute-start.18
  393.2 4.4 collective-permute-done.18
  397.6 2.0 fusion.161
  400.0 7.1 %multiply_reduce_fusion.8 = (f32[2048]{0:T(1024)}, f32[2048]{0:T(1024)}, f32[2048]{0:T(1024)}, f32[2048]{0:T(1024)}, f32[2048]{0:T(1024)}, /*index=5*/f32[2048]{...) fusion(f32[1,256,2048]{2,1,0:T(8,128)S(1)} %get-tuple-element.149, ...), kind=kLoop, calls=%fused_computation.295 | loop fusion | flops 25149440 | bytes 11641344 | tf_op jit(solution)/shard_map/reduce_sum | solution.py:111
  407.1 1.0 copy-done.33
  408.7 1.3 collective-permute-start.19
  410.0 1.7 stack.67
  412.6 2.5 psum.28
  415.1 11.2 %psum.29 = bf16[2,2048]{1,0:T(2,128)(2,1)S(1)} all-reduce(bf16[2,2048]{1,0:T(2,128)(2,1)S(1)} %psum.28), channel_id=1, replica_groups=mesh['groups'=2,'seq'=4,'tensor'=2,'dp'=2] {'seq'}, use_global_device_ids=true, to_apply=%region_29.30 | all-reduce | flops 4096 | bytes 16384 | tf_op jit(solution)/shard_map/psum | solution.py:139
  427.9 26.9 %all-reduce = (bf16[2,2048]{1,0:T(2,128)(2,1)S(1)}, bf16[13,2048]{1,0:T(8,128)(2,1)S(1)}) all-reduce(bf16[2,2048]{1,0:T(2,128)(2,1)S(1)} %fusion.170, bf16[13,2048]{1,0:T(8,128)(2,1)S(1)} %multiply_convert_fusion.3), channel_id=1, replica_groups=mesh['groups'=2,'seq'=4,'tensor'=2,'dp'=2] {'seq','dp'}, use_global_device_ids=true, to_apply=%region_54.55 | all-reduce | flops 30720 | bytes 122880 | tf_op jit(solution)/shard_map/psum | solution.py:140
  454.8 1.6 slice.349
  458.3 1.7 add_convert_fusion
  460.1 3.9 copy.14
  (354 shorter events, 22.0 us)
Async XLA Ops:
  7.2 149.4 %all-gather.2.cloned.1.call-start = ((), (), s32[]{:S(2)}) async-start(), calls=%async_computation.3 | async-start | bytes 3145728 | tf_op jit(solution)/shard_map/all_gather | solution.py:86
  8.0 8.0 %collective-permute-start = (bf16[1,1,2048]{2,1,0:T(2,128)(2,1)S(1)}, bf16[1,1,2048]{2,1,0:T(2,128)(2,1)S(1)}, u32[]{:S(2)}, u32[]{:S(2)}) collective-permute-start(bf16[1,1,2048]{2,1,0:T(2,128)(2,1)S(1)} %slice.100), channel_id=1, source_target_pairs={{0,4},{4,8},{8,12},{1,5},{5,9},{9,13},{2,6},{6,10},{10,14},{3,7},{... | collective-permute-start | bytes 12296 | tf_op jit(solution)/shard_map/ppermute | solution.py:13
  16.0 46.4 %copy-start.133 = (pred[256]{0:T(512)(128)(4,1)}, pred[256]{0:T(512)(128)(4,1)S(1)}, u32[]{:S(2)}) copy-start(pred[256]{0:T(512)(128)(4,1)S(1)} %get-tuple-element.141) | copy-start | bytes 772
  16.0 60.2 %copy-start.121 = (pred[256]{0:T(512)(128)(4,1)}, pred[256]{0:T(512)(128)(4,1)S(1)}, u32[]{:S(2)}) copy-start(pred[256]{0:T(512)(128)(4,1)S(1)} %get-tuple-element.140) | copy-start | bytes 772
  18.3 111.4 %copy-start = (bf16[1,256,2048]{2,1,0:T(8,128)(2,1)}, bf16[1,256,2048]{2,1,0:T(8,128)(2,1)S(1)}, u32[]{:S(2)}) copy-start(bf16[1,256,2048]{2,1,0:T(8,128)(2,1)S(1)} %fusion.18) | copy-start | bytes 3145732
  18.3 4.8 %collective-permute-start.1 = (bf16[1,2,2048]{2,1,0:T(2,128)(2,1)S(1)}, bf16[1,2,2048]{2,1,0:T(2,128)(2,1)S(1)}, u32[]{:S(2)}, u32[]{:S(2)}) collective-permute-start(bf16[1,2,2048]{2,1,0:T(2,128)(2,1)S(1)} %slice.147), channel_id=1, source_target_pairs={{0,4},{4,8},{8,12},{1,5},{5,9},{9,13},{2,6},{6,10},{10,14},{3,7},{... | collective-permute-start | bytes 24584 | tf_op jit(solution)/shard_map/ppermute | solution.py:13
  23.9 5.6 %collective-permute-start.2 = (bf16[1,4,2048]{2,1,0:T(4,128)(2,1)S(1)}, bf16[1,4,2048]{2,1,0:T(4,128)(2,1)S(1)}, u32[]{:S(2)}, u32[]{:S(2)}) collective-permute-start(bf16[1,4,2048]{2,1,0:T(4,128)(2,1)S(1)} %slice.149), channel_id=1, source_target_pairs={{0,4},{4,8},{8,12},{1,5},{5,9},{9,13},{2,6},{6,10},{10,14},{3,7},{... | collective-permute-start | bytes 49160 | tf_op jit(solution)/shard_map/ppermute | solution.py:13
  30.3 5.8 %collective-permute-start.3 = (bf16[1,8,2048]{2,1,0:T(8,128)(2,1)S(1)}, bf16[1,8,2048]{2,1,0:T(8,128)(2,1)S(1)}, u32[]{:S(2)}, u32[]{:S(2)}) collective-permute-start(bf16[1,8,2048]{2,1,0:T(8,128)(2,1)S(1)} %slice.151), channel_id=1, source_target_pairs={{0,4},{4,8},{8,12},{1,5},{5,9},{9,13},{2,6},{6,10},{10,14},{3,7},{... | collective-permute-start | bytes 98312 | tf_op jit(solution)/shard_map/ppermute | solution.py:13
  36.7 6.1 %collective-permute-start.4 = (bf16[1,16,2048]{2,1,0:T(8,128)(2,1)S(1)}, bf16[1,16,2048]{2,1,0:T(8,128)(2,1)S(1)}, u32[]{:S(2)}, u32[]{:S(2)}) collective-permute-start(bf16[1,16,2048]{2,1,0:T(8,128)(2,1)S(1)} %slice.153), channel_id=1, source_target_pairs={{0,4},{4,8},{8,12},{1,5},{5,9},{9,13},{2,6},{6,10},{10,14},{3,7},{... | collective-permute-start | bytes 196616 | tf_op jit(solution)/shard_map/ppermute | solution.py:13
  43.4 7.8 %collective-permute-start.5 = (bf16[1,32,2048]{2,1,0:T(8,128)(2,1)S(1)}, bf16[1,32,2048]{2,1,0:T(8,128)(2,1)S(1)}, u32[]{:S(2)}, u32[]{:S(2)}) collective-permute-start(bf16[1,32,2048]{2,1,0:T(8,128)(2,1)S(1)} %slice.155), channel_id=1, source_target_pairs={{0,4},{4,8},{8,12},{1,5},{5,9},{9,13},{2,6},{6,10},{10,14},{3,7},{... | collective-permute-start | bytes 393224 | tf_op jit(solution)/shard_map/ppermute | solution.py:13
  51.8 10.5 %collective-permute-start.6 = (bf16[1,64,2048]{2,1,0:T(8,128)(2,1)S(1)}, bf16[1,64,2048]{2,1,0:T(8,128)(2,1)S(1)}, u32[]{:S(2)}, u32[]{:S(2)}) collective-permute-start(bf16[1,64,2048]{2,1,0:T(8,128)(2,1)S(1)} %slice.157), channel_id=1, source_target_pairs={{0,4},{4,8},{8,12},{1,5},{5,9},{9,13},{2,6},{6,10},{10,14},{3,7},{... | collective-permute-start | bytes 786440 | tf_op jit(solution)/shard_map/ppermute | solution.py:13
  63.0 13.2 %collective-permute-start.7 = (bf16[1,128,2048]{2,1,0:T(8,128)(2,1)S(1)}, bf16[1,128,2048]{2,1,0:T(8,128)(2,1)S(1)}, u32[]{:S(2)}, u32[]{:S(2)}) collective-permute-start(bf16[1,128,2048]{2,1,0:T(8,128)(2,1)S(1)} %get-tuple-element.119), channel_id=1, source_target_pairs={{0,4},{4,8},{8,12},{1,5},{5,9},{9,13},{2,6},{6,10},{10,14},{3,7},{... | collective-permute-start | bytes 1572872 | tf_op jit(solution)/shard_map/ppermute | solution.py:13
  77.7 52.0 %copy-start.2 = (bf16[1,256,2048]{2,1,0:T(8,128)(2,1)S(1)}, bf16[1,256,2048]{2,1,0:T(8,128)(2,1)}, u32[]{:S(2)}) copy-start(bf16[1,256,2048]{2,1,0:T(8,128)(2,1)} %param.7) | copy-start | bytes 3145732
  77.7 20.4 %collective-permute-start.8 = (bf16[1,256,2048]{2,1,0:T(8,128)(2,1)}, bf16[1,256,2048]{2,1,0:T(8,128)(2,1)}, u32[]{:S(2)}, u32[]{:S(2)}) collective-permute-start(bf16[1,256,2048]{2,1,0:T(8,128)(2,1)} %fusion.52), channel_id=1, source_target_pairs={{0,4},{4,8},{8,12},{1,5},{5,9},{9,13},{2,6},{6,10},{10,14},{3,7},{... | collective-permute-start | bytes 3145736 | tf_op jit(solution)/shard_map/ppermute | solution.py:13
  83.3 316.4 %reduce-scatter.3.cloned.1.call-start = ((), (), s32[]{:S(2)}) async-start(), calls=%async_computation.2 | async-start | bytes 3145728 | tf_op jit(solution)/shard_map/reduce_scatter | solution.py:82
  83.4 46.3 %copy-start.5 = (bf16[1,256,2048]{2,1,0:T(8,128)(2,1)S(1)}, bf16[1,256,2048]{2,1,0:T(8,128)(2,1)}, u32[]{:S(2)}) copy-start(bf16[1,256,2048]{2,1,0:T(8,128)(2,1)} %copy-done.4) | copy-start | bytes 3145732
  83.4 46.3 %copy-start.8 = (bf16[1,256,2048]{2,1,0:T(8,128)(2,1)S(1)}, bf16[1,256,2048]{2,1,0:T(8,128)(2,1)}, u32[]{:S(2)}) copy-start(bf16[1,256,2048]{2,1,0:T(8,128)(2,1)} %copy-done.7) | copy-start | bytes 3145732
  83.4 46.3 %copy-start.11 = (bf16[1,256,2048]{2,1,0:T(8,128)(2,1)S(1)}, bf16[1,256,2048]{2,1,0:T(8,128)(2,1)}, u32[]{:S(2)}) copy-start(bf16[1,256,2048]{2,1,0:T(8,128)(2,1)} %copy-done.10) | copy-start | bytes 3145732
  83.4 46.3 %copy-start.46 = (bf16[1,16,2048]{2,1,0:T(8,128)(2,1)S(1)}, bf16[1,16,2048]{2,1,0:T(8,128)(2,1)}, u32[]{:S(2)}) copy-start(bf16[1,16,2048]{2,1,0:T(8,128)(2,1)} %copy-done.45) | copy-start | bytes 196612
  83.4 46.3 %copy-start.49 = (bf16[1,8,2048]{2,1,0:T(8,128)(2,1)S(1)}, bf16[1,8,2048]{2,1,0:T(8,128)(2,1)}, u32[]{:S(2)}) copy-start(bf16[1,8,2048]{2,1,0:T(8,128)(2,1)} %copy-done.48) | copy-start | bytes 98308
  83.4 46.3 %copy-start.52 = (bf16[1,4,2048]{2,1,0:T(4,128)(2,1)S(1)}, bf16[1,4,2048]{2,1,0:T(4,128)(2,1)}, u32[]{:S(2)}) copy-start(bf16[1,4,2048]{2,1,0:T(4,128)(2,1)} %copy-done.51) | copy-start | bytes 49156
  83.4 46.3 %copy-start.65 = (bf16[1,1,2048]{2,1,0:T(2,128)(2,1)S(1)}, bf16[1,1,2048]{2,1,0:T(2,128)(2,1)}, u32[]{:S(2)}) copy-start(bf16[1,1,2048]{2,1,0:T(2,128)(2,1)} %copy-done.64) | copy-start | bytes 12292
  83.4 46.3 %copy-start.68 = (bf16[1,2,2048]{2,1,0:T(2,128)(2,1)S(1)}, bf16[1,2,2048]{2,1,0:T(2,128)(2,1)}, u32[]{:S(2)}) copy-start(bf16[1,2,2048]{2,1,0:T(2,128)(2,1)} %copy-done.67) | copy-start | bytes 24580
  83.4 46.3 %copy-start.116 = (pred[256]{0:T(512)(128)(4,1)S(1)}, pred[256]{0:T(512)(128)(4,1)}, u32[]{:S(2)}) copy-start(pred[256]{0:T(512)(128)(4,1)} %copy-done.115) | copy-start | bytes 772
  83.5 46.3 %copy-start.119 = (pred[256]{0:T(512)(128)(4,1)S(1)}, pred[256]{0:T(512)(128)(4,1)}, u32[]{:S(2)}) copy-start(pred[256]{0:T(512)(128)(4,1)} %copy-done.118) | copy-start | bytes 772
  83.5 46.3 %copy-start.122 = (pred[256]{0:T(512)(128)(4,1)S(1)}, pred[256]{0:T(512)(128)(4,1)}, u32[]{:S(2)}) copy-start(pred[256]{0:T(512)(128)(4,1)} %copy-done.121) | copy-start | bytes 772
  83.5 46.3 %copy-start.125 = (pred[256]{0:T(512)(128)(4,1)S(1)}, pred[256]{0:T(512)(128)(4,1)}, u32[]{:S(2)}) copy-start(pred[256]{0:T(512)(128)(4,1)} %copy-done.124) | copy-start | bytes 772
  83.5 46.3 %copy-start.128 = (pred[256]{0:T(512)(128)(4,1)S(1)}, pred[256]{0:T(512)(128)(4,1)}, u32[]{:S(2)}) copy-start(pred[256]{0:T(512)(128)(4,1)} %copy-done.127) | copy-start | bytes 772
  83.5 46.3 %copy-start.131 = (pred[256]{0:T(512)(128)(4,1)S(1)}, pred[256]{0:T(512)(128)(4,1)}, u32[]{:S(2)}) copy-start(pred[256]{0:T(512)(128)(4,1)} %copy-done.130) | copy-start | bytes 772
  83.5 46.3 %copy-start.134 = (pred[256]{0:T(512)(128)(4,1)S(1)}, pred[256]{0:T(512)(128)(4,1)}, u32[]{:S(2)}) copy-start(pred[256]{0:T(512)(128)(4,1)} %copy-done.133) | copy-start | bytes 772
  83.5 46.3 %copy-start.136 = (pred[256]{0:T(512)(128)(4,1)S(1)}, pred[256]{0:T(512)(128)(4,1)}, u32[]{:S(2)}) copy-start(pred[256]{0:T(512)(128)(4,1)} %get-tuple-element.139) | copy-start | bytes 772
  83.5 46.3 %copy-start.139 = (pred[256]{0:T(512)(128)(4,1)S(1)}, pred[256]{0:T(512)(128)(4,1)}, u32[]{:S(2)}) copy-start(pred[256]{0:T(512)(128)(4,1)} %copy-done.138) | copy-start | bytes 772
  83.5 46.3 %copy-start.141 = (pred[256]{0:T(512)(128)(4,1)S(1)}, pred[256]{0:T(512)(128)(4,1)}, u32[]{:S(2)}) copy-start(pred[256]{0:T(512)(128)(4,1)} %get-tuple-element.138) | copy-start | bytes 772
  100.2 29.5 %collective-permute-start.9 = (bf16[1,256,2048]{2,1,0:T(8,128)(2,1)S(1)}, bf16[1,256,2048]{2,1,0:T(8,128)(2,1)S(1)}, u32[]{:S(2)}, u32[]{:S(2)}) collective-permute-start(bf16[1,256,2048]{2,1,0:T(8,128)(2,1)S(1)} %fusion.57), channel_id=1, source_target_pairs={{0,8},{4,12},{1,9},{5,13},{2,10},{6,14},{3,11},{7,15},{16,24},{20,... | collective-permute-start | bytes 3145736 | tf_op jit(solution)/shard_map/ppermute | solution.py:13
  156.3 303.8 %reduce-scatter.5.cloned.1.call-start = ((), (), s32[]{:S(2)}) async-start(), calls=%async_computation.4 | async-start | bytes 18874368 | tf_op jit(solution)/shard_map/reduce_scatter | solution.py:88
  167.9 66.6 %copy-start.29 = (bf16[1,256,2048]{2,1,0:T(8,128)(2,1)S(1)}, bf16[1,256,2048]{2,1,0:T(8,128)(2,1)}, u32[]{:S(2)}) copy-start(bf16[1,256,2048]{2,1,0:T(8,128)(2,1)} %copy-done.28) | copy-start | bytes 3145732
  167.9 66.6 %copy-start.35 = (bf16[1,256,2048]{2,1,0:T(8,128)(2,1)S(1)}, bf16[1,256,2048]{2,1,0:T(8,128)(2,1)}, u32[]{:S(2)}) copy-start(bf16[1,256,2048]{2,1,0:T(8,128)(2,1)} %copy-done.34) | copy-start | bytes 3145732
  167.9 66.6 %copy-start.36 = (bf16[1,256,2048]{2,1,0:T(8,128)(2,1)S(1)}, bf16[1,256,2048]{2,1,0:T(8,128)(2,1)}, u32[]{:S(2)}) copy-start(bf16[1,256,2048]{2,1,0:T(8,128)(2,1)} %get-tuple-element.111) | copy-start | bytes 3145732
  168.0 66.6 %copy-start.40 = (f32[1,2048]{1,0:T(1,128)S(1)}, f32[1,2048]{1,0:T(1,128)}, u32[]{:S(2)}) copy-start(f32[1,2048]{1,0:T(1,128)} %copy-done.39) | copy-start | bytes 24580
  168.0 66.6 %copy-start.43 = (f32[1,2048]{1,0:T(1,128)S(1)}, f32[1,2048]{1,0:T(1,128)}, u32[]{:S(2)}) copy-start(f32[1,2048]{1,0:T(1,128)} %copy-done.42) | copy-start | bytes 24580
  168.0 66.6 %copy-start.63 = (f32[1,2048]{1,0:T(1,128)S(1)}, f32[1,2048]{1,0:T(1,128)}, u32[]{:S(2)}) copy-start(f32[1,2048]{1,0:T(1,128)} %copy-done.62) | copy-start | bytes 24580
  168.0 66.6 %copy-start.79 = (f32[2048]{0:T(1024)S(1)}, f32[2048]{0:T(1024)}, u32[]{:S(2)}) copy-start(f32[2048]{0:T(1024)} %copy-done.78) | copy-start | bytes 24580
  168.0 66.6 %copy-start.81 = (f32[2048]{0:T(1024)S(1)}, f32[2048]{0:T(1024)}, u32[]{:S(2)}) copy-start(f32[2048]{0:T(1024)} %copy-done.80) | copy-start | bytes 24580
  168.0 66.6 %copy-start.83 = (f32[1,2048]{1,0:T(1,128)S(1)}, f32[1,2048]{1,0:T(1,128)}, u32[]{:S(2)}) copy-start(f32[1,2048]{1,0:T(1,128)} %copy-done.82) | copy-start | bytes 24580
  168.0 66.6 %copy-start.85 = (f32[1,2048]{1,0:T(1,128)S(1)}, f32[1,2048]{1,0:T(1,128)}, u32[]{:S(2)}) copy-start(f32[1,2048]{1,0:T(1,128)} %copy-done.84) | copy-start | bytes 24580
  168.0 66.6 %copy-start.87 = (f32[1,2048]{1,0:T(1,128)S(1)}, f32[1,2048]{1,0:T(1,128)}, u32[]{:S(2)}) copy-start(f32[1,2048]{1,0:T(1,128)} %copy-done.86) | copy-start | bytes 24580
  168.0 66.6 %copy-start.89 = (f32[1,2048]{1,0:T(1,128)S(1)}, f32[1,2048]{1,0:T(1,128)}, u32[]{:S(2)}) copy-start(f32[1,2048]{1,0:T(1,128)} %copy-done.88) | copy-start | bytes 24580
  168.1 66.6 %copy-start.137 = (pred[256]{0:T(512)(128)(4,1)S(1)}, pred[256]{0:T(512)(128)(4,1)}, u32[]{:S(2)}) copy-start(pred[256]{0:T(512)(128)(4,1)} %get-tuple-element.139) | copy-start | bytes 772
  168.1 66.6 %copy-start.142 = (pred[256]{0:T(512)(128)(4,1)S(1)}, pred[256]{0:T(512)(128)(4,1)}, u32[]{:S(2)}) copy-start(pred[256]{0:T(512)(128)(4,1)} %get-tuple-element.138) | copy-start | bytes 772
  179.2 55.3 %collective-permute-start.10 = (bf16[1,256,2048]{2,1,0:T(8,128)(2,1)S(1)}, bf16[1,256,2048]{2,1,0:T(8,128)(2,1)S(1)}, u32[]{:S(2)}, u32[]{:S(2)}) collective-permute-start(bf16[1,256,2048]{2,1,0:T(8,128)(2,1)S(1)} %get-tuple-element.148), channel_id=1, source_target_pairs={{8,0},{12,4},{9,1},{13,5},{10,2},{14,6},{11,3},{15,7},{24,16},{28,... | collective-permute-start | bytes 3145736 | tf_op jit(solution)/shard_map/ppermute | solution.py:13
  243.1 50.8 %copy-start.27 = (bf16[1,128,2048]{2,1,0:T(8,128)(2,1)S(1)}, bf16[1,128,2048]{2,1,0:T(8,128)(2,1)}, u32[]{:S(2)}) copy-start(bf16[1,128,2048]{2,1,0:T(8,128)(2,1)} %copy-done.26) | copy-start | bytes 1572868
  243.1 50.8 %copy-start.32 = (bf16[1,128,2048]{2,1,0:T(8,128)(2,1)S(1)}, bf16[1,128,2048]{2,1,0:T(8,128)(2,1)}, u32[]{:S(2)}) copy-start(bf16[1,128,2048]{2,1,0:T(8,128)(2,1)} %copy-done.31) | copy-start | bytes 1572868
  243.1 50.8 %copy-start.123 = (pred[256]{0:T(512)(128)(4,1)S(1)}, pred[256]{0:T(512)(128)(4,1)}, u32[]{:S(2)}) copy-start(pred[256]{0:T(512)(128)(4,1)} %copy-done.121) | copy-start | bytes 772
  243.6 51.3 %copy-start.61 = (f32[1,2048]{1,0:T(1,128)S(1)}, f32[1,2048]{1,0:T(1,128)}, u32[]{:S(2)}) copy-start(f32[1,2048]{1,0:T(1,128)} %copy-done.60) | copy-start | bytes 24580
  243.6 50.3 %collective-permute-start.11 = (bf16[1,256,2048]{2,1,0:T(8,128)(2,1)S(1)}, bf16[1,256,2048]{2,1,0:T(8,128)(2,1)S(1)}, u32[]{:S(2)}, u32[]{:S(2)}) collective-permute-start(bf16[1,256,2048]{2,1,0:T(8,128)(2,1)S(1)} %fusion.96), channel_id=1, source_target_pairs={{4,0},{8,4},{12,8},{5,1},{9,5},{13,9},{6,2},{10,6},{14,10},{7,3},{... | collective-permute-start | bytes 3145736 | tf_op jit(solution)/shard_map/ppermute | solution.py:13
  295.5 26.7 %collective-permute-start.12 = (bf16[1,128,2048]{2,1,0:T(8,128)(2,1)S(1)}, bf16[1,128,2048]{2,1,0:T(8,128)(2,1)S(1)}, u32[]{:S(2)}, u32[]{:S(2)}) collective-permute-start(bf16[1,128,2048]{2,1,0:T(8,128)(2,1)S(1)} %get-tuple-element.118), channel_id=1, source_target_pairs={{4,0},{8,4},{12,8},{5,1},{9,5},{13,9},{6,2},{10,6},{14,10},{7,3},{... | collective-permute-start | bytes 1572872 | tf_op jit(solution)/shard_map/ppermute | solution.py:13
  328.3 16.1 %collective-permute-start.13 = (bf16[1,64,2048]{2,1,0:T(8,128)(2,1)S(1)}, bf16[1,64,2048]{2,1,0:T(8,128)(2,1)S(1)}, u32[]{:S(2)}, u32[]{:S(2)}) collective-permute-start(bf16[1,64,2048]{2,1,0:T(8,128)(2,1)S(1)} %slice.164), channel_id=1, source_target_pairs={{4,0},{8,4},{12,8},{5,1},{9,5},{13,9},{6,2},{10,6},{14,10},{7,3},{... | collective-permute-start | bytes 786440 | tf_op jit(solution)/shard_map/ppermute | solution.py:13
  345.9 10.7 %collective-permute-start.14 = (bf16[1,32,2048]{2,1,0:T(8,128)(2,1)S(1)}, bf16[1,32,2048]{2,1,0:T(8,128)(2,1)S(1)}, u32[]{:S(2)}, u32[]{:S(2)}) collective-permute-start(bf16[1,32,2048]{2,1,0:T(8,128)(2,1)S(1)} %slice.166), channel_id=1, source_target_pairs={{4,0},{8,4},{12,8},{5,1},{9,5},{13,9},{6,2},{10,6},{14,10},{7,3},{... | collective-permute-start | bytes 393224 | tf_op jit(solution)/shard_map/ppermute | solution.py:13
  361.4 8.4 %collective-permute-start.15 = (bf16[1,16,2048]{2,1,0:T(8,128)(2,1)S(1)}, bf16[1,16,2048]{2,1,0:T(8,128)(2,1)S(1)}, u32[]{:S(2)}, u32[]{:S(2)}) collective-permute-start(bf16[1,16,2048]{2,1,0:T(8,128)(2,1)S(1)} %slice.168), channel_id=1, source_target_pairs={{4,0},{8,4},{12,8},{5,1},{9,5},{13,9},{6,2},{10,6},{14,10},{7,3},{... | collective-permute-start | bytes 196616 | tf_op jit(solution)/shard_map/ppermute | solution.py:13
  371.3 7.0 %collective-permute-start.16 = (bf16[1,8,2048]{2,1,0:T(8,128)(2,1)S(1)}, bf16[1,8,2048]{2,1,0:T(8,128)(2,1)S(1)}, u32[]{:S(2)}, u32[]{:S(2)}) collective-permute-start(bf16[1,8,2048]{2,1,0:T(8,128)(2,1)S(1)} %slice.170), channel_id=1, source_target_pairs={{4,0},{8,4},{12,8},{5,1},{9,5},{13,9},{6,2},{10,6},{14,10},{7,3},{... | collective-permute-start | bytes 98312 | tf_op jit(solution)/shard_map/ppermute | solution.py:13
  383.4 6.5 %collective-permute-start.17 = (bf16[1,4,2048]{2,1,0:T(4,128)(2,1)S(1)}, bf16[1,4,2048]{2,1,0:T(4,128)(2,1)S(1)}, u32[]{:S(2)}, u32[]{:S(2)}) collective-permute-start(bf16[1,4,2048]{2,1,0:T(4,128)(2,1)S(1)} %slice.172), channel_id=1, source_target_pairs={{4,0},{8,4},{12,8},{5,1},{9,5},{13,9},{6,2},{10,6},{14,10},{7,3},{... | collective-permute-start | bytes 49160 | tf_op jit(solution)/shard_map/ppermute | solution.py:13
  391.5 6.1 %collective-permute-start.18 = (bf16[1,2,2048]{2,1,0:T(2,128)(2,1)S(1)}, bf16[1,2,2048]{2,1,0:T(2,128)(2,1)S(1)}, u32[]{:S(2)}, u32[]{:S(2)}) collective-permute-start(bf16[1,2,2048]{2,1,0:T(2,128)(2,1)S(1)} %slice.348), channel_id=1, source_target_pairs={{4,0},{8,4},{12,8},{5,1},{9,5},{13,9},{6,2},{10,6},{14,10},{7,3},{... | collective-permute-start | bytes 24584 | tf_op jit(solution)/shard_map/ppermute | solution.py:13
  407.1 51.2 %copy-start.30 = (bf16[1,256,2048]{2,1,0:T(8,128)(2,1)S(1)}, bf16[1,256,2048]{2,1,0:T(8,128)(2,1)}, u32[]{:S(2)}) copy-start(bf16[1,256,2048]{2,1,0:T(8,128)(2,1)} %get-tuple-element.108) | copy-start | bytes 3145732
  408.7 49.7 %collective-permute-start.19 = (bf16[1,1,2048]{2,1,0:T(2,128)(2,1)}, bf16[1,1,2048]{2,1,0:T(2,128)(2,1)S(1)}, u32[]{:S(2)}, u32[]{:S(2)}) collective-permute-start(bf16[1,1,2048]{2,1,0:T(2,128)(2,1)} %slice.350), channel_id=1, source_target_pairs={{4,0},{8,4},{12,8},{5,1},{9,5},{13,9},{6,2},{10,6},{14,10},{7,3},{... | collective-permute-start | bytes 12296 | tf_op jit(solution)/shard_map/ppermute | solution.py:13
  (102 other events, 1521.0 us)
Sparse Core Ops, SparseCore 0:
  83.4 32.3 all-gather.1
  156.4 45.6 reduce-scatter.2
  204.6 213.1 reduce-scatter.4
